TPU v7x, 256 devices: a whole 4x4x8 slice. The times are simulated.
256 devices in a mesh: blk: 32 (over y_hi, z, core), col: 8 (over y_lo, x).
Axes of the slice: x: 4, y: 4 (y_hi: 2, y_lo: 2; y = y_hi * 2 + y_lo), z: 8, core: 2. Of those that a mesh axis runs over, the one named last changes fastest.
Arguments:
- a_blocks: float32 [32, 128, 384, 128], P('col', None, 'blk'), may hold values from -6 to 6
- a_mask: int32 [32, 384], P('col', 'blk'), may hold values 0 or 1
- b_blocks: float32 [384, 128, 32, 128], P('blk', None, 'col'), may hold values from -0.0546875 to 0.0546875
- b_mask: int32 [384, 32], P('blk', 'col'), may hold values 0 or 1
- c_mask: int32 [32, 32], P('blk', 'col'), may hold values 0 or 1
Outputs:
- product: float32 [32, 128, 32, 128], P('blk', None, 'col')
All inputs are finite; a program needn't handle non-finite values. No bound on the sum of `a_mask` or of `b_mask` or of `c_mask` on one device may be relied on, other than what follows from the above.
Results may differ from a plain program's by a relative error of at most 0.000071.
Values sent between devices are 32-bit elements; how exact they have to be, the bound alone decides.
No kernel may reach another device: no remote copies, remote signals or barrier semaphores. Data moves between devices by JAX's collectives and lax.ppermute only.
A program may use at most 128 MiB of HBM per device.

v0:
```python
import jax
import jax.numpy as jnp
from jax import lax
from jax.sharding import PartitionSpec as P


def shards(a_blocks, a_mask, b_blocks, b_mask, c_mask):
    masked_a = a_blocks * a_mask.astype(jnp.float32)[:, None, :, None]
    masked_b = b_blocks * b_mask.astype(jnp.float32)[:, None, :, None]
    col_count = masked_b.shape[2]
    block_side = masked_b.shape[3]
    flat_b = masked_b.reshape(masked_b.shape[0] * masked_b.shape[1], col_count * block_side)
    piece = lax.all_gather(masked_a, "col", axis=0, tiled=True)
    count = piece.shape[0]
    flat_piece = piece.reshape(count * piece.shape[1], piece.shape[2] * piece.shape[3])
    result = jnp.dot(
        flat_piece, flat_b, precision=lax.Precision.HIGHEST, preferred_element_type=jnp.float32
    )
    partial_value = result.reshape(count, piece.shape[1], col_count, block_side)
    owned = lax.psum_scatter(partial_value, "blk", scatter_dimension=0, tiled=True)
    return owned * c_mask.astype(jnp.float32)[:, None, :, None]


def solution(mesh):
    return jax.shard_map(
        shards,
        mesh=mesh,
        in_specs=(
            P("col", None, "blk", None),
            P("col", "blk"),
            P("blk", None, "col", None),
            P("blk", "col"),
            P("blk", "col"),
        ),
        out_specs=P("blk", None, "col", None),
        check_vma=False,
    )
```

profile of v0, /device:TPU:2, one launch (start us, length us, event | category | flops | bytes accessed | tf_op | source)
XLA Modules:
  0.0 535.6 jit_solution(895382643046142250)
XLA Ops:
  6.5 0.0 all-gather.2.cloned.1.call-start
  6.5 0.7 convert_element_type.9
  7.2 3.9 broadcast_multiply_fusion.1
  11.1 0.0 copy-start.2
  11.1 0.0 copy-start
  11.1 0.0 all-gather.2.cloned.1.call-update
  11.1 0.0 reduce-scatter.2.cloned.1.call-start
  11.2 0.6 copy-done.2
  11.8 0.1 copy.16
  11.9 1.1 copy-done
  13.0 0.7 broadcast_multiply_fusion
  13.7 0.3 copy.25
  14.1 2.3 copy.17
  16.4 0.0 copy-start.1
  16.4 247.4 %all-gather.2.cloned.1.call-done = f32[32,128,12,128]{3,1,2,0:T(8,128)} async-done(((f32[4,128,12,128]{3,1,2,0:T(8,128)}), f32[32,128,12,128]{3,1,2,0:T(8,128)}) %all-gather.2.cloned.1.call-update) | async-done | bytes 25165840 | tf_op jit(solution)/shard_map/all_gather | solution.py:13
  263.7 24.6 %copy.15 = f32[32,128,12,128]{1,3,2,0:T(8,128)} copy(f32[32,128,12,128]{3,1,2,0:T(8,128)} %all-gather.2.cloned.1.call-done) | data formatting | bytes 50331648 | tf_op jit(solution)/shard_map/all_gather | solution.py:13
  288.4 0.0 copy-done.1
  288.4 82.6 %fusion = f32[32,128,4,128]{3,1,2,0:T(8,128)} fusion(f32[32,128,1536,1]{1,2,3,0:T(8,128)} %bitcast.20, f32[4,128,1536,1]{2,1,0,3:T(8,128)S(1)} %bitcast.23), kind=kOutput, calls=%fused_computation.5 | convolution fusion | flops 38654705664 | bytes 36700160 | tf_op jit(solution)/shard_map/dot_general | solution.py:16
  371.0 0.0 copy-start.3
  371.0 0.0 reduce-scatter.2.cloned.1.call-update
  371.0 0.6 copy-done.3
  371.6 155.2 %reduce-scatter.2.cloned.1.call-done = f32[1,128,4,128]{3,1,2,0:T(8,128)} async-done(((f32[32,128,4,128]{3,1,2,0:T(8,128)}), f32[1,128,4,128]{3,1,2,0:T(8,128)}) %reduce-scatter.2.cloned.1.call-update) | async-done | bytes 262160 | tf_op jit(solution)/shard_map/reduce_scatter | solution.py:20
  526.8 1.0 broadcast_multiply_fusion.2
  527.9 0.9 copy.19
  (2 shorter events, 0.0 us)
Async XLA Ops:
  6.5 257.2 %all-gather.2.cloned.1.call-start = ((), (), s32[]{:S(2)}) async-start(), calls=%async_computation.1 | async-start | bytes 28311552 | tf_op jit(solution)/shard_map/all_gather | solution.py:13
  11.1 0.7 copy-start.2
  11.1 1.9 copy-start
  11.1 515.7 %reduce-scatter.2.cloned.1.call-start = ((), (), s32[]{:S(2)}) async-start(), calls=%async_computation.2 | async-start | bytes 8650752 | tf_op jit(solution)/shard_map/reduce_scatter | solution.py:20
  16.4 272.0 %copy-start.1 = (f32[512,1536]{1,0:T(8,128)S(1)}, f32[512,1536]{1,0:T(8,128)}, u32[]{:S(2)}) copy-start(f32[512,1536]{1,0:T(8,128)} %copy.17) | copy-start | bytes 9437188
  371.0 0.7 copy-start.3
Sparse Core Ops, SparseCore 0:
  11.3 252.4 all-gather.1
  371.1 155.6 reduce-scatter.1
where the time goes:
time: 536 us
  waiting for transfers between devices  403 us (75%)
  matrix products  82.6 us (15%)
  local copies, waits for them, and re-layouts  30.6 us (6%)
  between operations  13.4 us (2%)
  other arithmetic  6.34 us (1%)
    all_gather x1, waiting for transfers between devices, shards(): piece = lax.all_gather(masked_a, 'col', axis=0, tiled=True)  247 us
    reduce_scatter x1, waiting for transfers between devices, shards(): lax.psum_scatter(partial_value, 'blk', scatter_dimension=0, tiled=True)  155 us
    dot_general x1, matrix products, shards(): jnp.dot(flat_piece, flat_b, precision=lax.Precision.HIGHEST, preferred_el...  82.6 us
    all_gather x1, local copies, waits for them, and re-layouts, shards(): piece = lax.all_gather(masked_a, 'col', axis=0, tiled=True)  24.6 us
  transfers between devices with their start and end apart: 2, of which 2 were waited for; matrix products, arithmetic and copies ran while one was open for 1% of the time, Pallas kernels for 0%

commit v1 on v0

--- a/solution.py
+++ b/solution.py
@@ -10,7 +10,9 @@
     col_count = masked_b.shape[2]
     block_side = masked_b.shape[3]
     flat_b = masked_b.reshape(masked_b.shape[0] * masked_b.shape[1], col_count * block_side)
-    piece = lax.all_gather(masked_a, "col", axis=0, tiled=True)
+    piece = jnp.concatenate(
+        lax.all_to_all(jnp.stack([masked_a] * lax.axis_size("col")), "col", 0, 0), axis=0
+    )
     count = piece.shape[0]
     flat_piece = piece.reshape(count * piece.shape[1], piece.shape[2] * piece.shape[3])
     result = jnp.dot(

time: 536 us -> 658 us (1.23)
  waiting for transfers between devices: 403 us -> 528 us
  local copies, waits for them, and re-layouts: 30.6 us -> 18.1 us
  starting transfers between devices: 0.04 us -> 8.81 us
    all_to_all x0 -> x1, waiting for transfers between devices: none -> 366 us  [shards(): lax.all_to_all(jnp.stack([masked_a] * lax.axis_size('col')), 'col', 0, 0)]
    all_gather x1 -> x0, waiting for transfers between devices: 247 us -> none  [shards(): piece = lax.all_gather(masked_a, 'col', axis=0, tiled=True)]
    all_gather x1 -> x0, local copies, waits for them, and re-layouts: 24.6 us -> none  [shards(): piece = lax.all_gather(masked_a, 'col', axis=0, tiled=True)]
    another operation x0 -> x1, local copies, waits for them, and re-layouts: none -> 11.5 us  [shards(): jnp.stack([masked_a] * lax.axis_size('col'))]
    all_to_all x0 -> x1, starting transfers between devices: none -> 8.81 us  [shards(): lax.all_to_all(jnp.stack([masked_a] * lax.axis_size('col')), 'col', 0, 0)]
    reduce_scatter x1, waiting for transfers between devices: 155 us -> 162 us  [shards(): lax.psum_scatter(partial_value, 'blk', scatter_dimension=0, tiled=True)]
where the time goes in v1:
time: 658 us
  waiting for transfers between devices  528 us (80%)
  matrix products  83.5 us (13%)
  local copies, waits for them, and re-layouts  18.1 us (3%)
  between operations  13.4 us (2%)
  starting transfers between devices  8.81 us (1%)
    all_to_all x1, waiting for transfers between devices, shards(): lax.all_to_all(jnp.stack([masked_a] * lax.axis_size('col')), 'col', 0, 0)  366 us
    reduce_scatter x1, waiting for transfers between devices, shards(): lax.psum_scatter(partial_value, 'blk', scatter_dimension=0, tiled=True)  162 us
    dot_general x1, matrix products, shards(): jnp.dot(flat_piece, flat_b, precision=lax.Precision.HIGHEST, preferred_el...  83.5 us
  transfers between devices with their start and end apart: 2, of which 2 were waited for; matrix products, arithmetic and copies ran while one was open for 1% of the time, Pallas kernels for 0%

profile of v1, /device:TPU:2, one launch (start us, length us, event | category | flops | bytes accessed | tf_op | source)
XLA Modules:
  0.0 658.0 jit_solution(3522056019874554176)
XLA Ops:
  6.5 0.7 convert_element_type.9
  7.2 3.8 broadcast_multiply_fusion.1
  11.0 2.4 copy.10
  13.4 11.5 %stack.2 = f32[8,4,128,12,128]{2,4,3,1,0:T(8,128)} broadcast(f32[4,128,12,128]{1,3,2,0:T(8,128)S(1)} %copy.10), dimensions={1,2,3,4} | broadcast | bytes 28311552 | tf_op jit(solution)/shard_map/stack | solution.py:14
  24.9 0.0 copy-start.1
  24.9 0.0 copy-start
  24.9 8.8 %all-to-all-start = ((f32[8,4,128,12,128]{2,4,3,1,0:T(8,128)}), f32[8,4,128,12,128]{2,4,3,1,0:T(8,128)}, u32[]{:S(2)}, u32[]{:S(2)}) async-start(f32[8,4,128,12,128]{2,4,3,1,0:T(8,128)} %stack.2), calls=%async_computation | async-start | bytes 50331648 | tf_op jit(solution)/shard_map/all_to_all | solution.py:14
  33.7 0.0 reduce-scatter.2.cloned.1.call-start
  33.7 0.0 copy-done.1
  33.7 0.1 copy.11
  33.8 0.0 copy-done
  33.8 0.7 broadcast_multiply_fusion
  34.6 0.3 copy.20
  34.9 2.3 copy.12
  37.2 365.7 %all-to-all-done = f32[8,4,128,12,128]{2,4,3,1,0:T(8,128)} async-done(((f32[8,4,128,12,128]{2,4,3,1,0:T(8,128)}), f32[8,4,128,12,128]{2,4,3,1,0:T(8,128)}, u32[]{:S(2)}, u32[]{:S(2)}) %all-to-all-start) | async-done | bytes 25165856 | tf_op jit(solution)/shard_map/all_to_all | solution.py:14
  402.9 83.5 %fusion = f32[32,128,4,128]{3,1,2,0:T(8,128)} fusion(f32[32,128,1536,1]{1,2,3,0:T(8,128)} %bitcast.7, f32[4,128,1536,1]{2,1,0,3:T(8,128)} %bitcast.22), kind=kOutput, calls=%fused_computation.5 | convolution fusion | flops 38654705664 | bytes 36700160 | tf_op jit(solution)/shard_map/dot_general | solution.py:18
  486.4 0.0 copy-start.2
  486.4 0.0 reduce-scatter.2.cloned.1.call-update
  486.4 0.6 copy-done.2
  487.1 162.1 %reduce-scatter.2.cloned.1.call-done = f32[1,128,4,128]{3,1,2,0:T(8,128)} async-done(((f32[32,128,4,128]{3,1,2,0:T(8,128)}), f32[1,128,4,128]{3,1,2,0:T(8,128)}) %reduce-scatter.2.cloned.1.call-update) | async-done | bytes 262160 | tf_op jit(solution)/shard_map/reduce_scatter | solution.py:22
  649.2 1.0 broadcast_multiply_fusion.2
  650.2 0.9 copy.14
  (2 shorter events, 0.0 us)
Async XLA Ops:
  24.9 8.8 %copy-start.1 = (s32[12,4]{0,1:T(4,128)S(1)}, s32[12,4]{0,1:T(4,128)}, u32[]{:S(2)}) copy-start(s32[12,4]{0,1:T(4,128)} %param.8) | copy-start | bytes 580
  24.9 8.9 %copy-start = (f32[12,128,4,128]{3,2,1,0:T(4,128)S(1)}, f32[12,128,4,128]{3,2,1,0:T(4,128)}, u32[]{:S(2)}) copy-start(f32[12,128,4,128]{3,2,1,0:T(4,128)} %param.7) | copy-start | bytes 9437188
  24.9 378.0 %all-to-all-start = ((f32[8,4,128,12,128]{2,4,3,1,0:T(8,128)}), f32[8,4,128,12,128]{2,4,3,1,0:T(8,128)}, u32[]{:S(2)}, u32[]{:S(2)}) async-start(f32[8,4,128,12,128]{2,4,3,1,0:T(8,128)} %stack.2), calls=%async_computation | async-start | bytes 50331648 | tf_op jit(solution)/shard_map/all_to_all | solution.py:14
  33.7 615.5 %reduce-scatter.2.cloned.1.call-start = ((), (), s32[]{:S(2)}) async-start(), calls=%async_computation.2 | async-start | bytes 8650752 | tf_op jit(solution)/shard_map/reduce_scatter | solution.py:22
  486.4 0.7 copy-start.2
Sparse Core Ops, SparseCore 0:
  486.6 162.5 reduce-scatter.1
